TPU v7x, 256 devices: a whole 4x4x8 slice. The times are simulated.
256 devices in a mesh: ctx: 64 (over y, z, core), head: 4 (over x).
Axes of the slice: x: 4, y: 4, z: 8, core: 2. Of those that a mesh axis runs over, the one named last changes fastest.
Arguments:
- queries: bfloat16 [8192, 4096], P('ctx', 'head'), may hold values from -6 to 6
- key_heads: bfloat16 [8192, 4096], P('ctx', 'head'), may hold values from -0.59765625 to 0.59765625
- value_heads: bfloat16 [8192, 4096], P('ctx', 'head'), may hold values from -12 to 12
- gate_logits: bfloat16 [8192, 4096], P('ctx', 'head'), may hold values from -9 to 9
- log_decay: float32 [8192, 32], P('ctx', 'head'), may hold values from -2 to 0
- attn_gain: float32 [4096], P('head'), may hold values from 0.25 to 1.75
- out_weight: bfloat16 [32, 128, 6144], P('head', 'ctx'), may hold values from -0.09375 to 0.09375
- residual: bfloat16 [8192, 6144], P('ctx'), may hold values from -24 to 24
- norm_gain: float32 [6144], replicated, may hold values from 0.25 to 1.75
- router_weight: bfloat16 [6144, 32], replicated, may hold values from -0.078125 to 0.078125
- expert_ids: int32 [8192, 2], P('ctx'), may hold values from 0 to 31, as said below
- expert_gate: bfloat16 [36864, 6144], P(('ctx', 'head')), may hold values from -0.078125 to 0.078125
- expert_up: bfloat16 [36864, 6144], P(('ctx', 'head')), may hold values from -0.078125 to 0.078125
- expert_down: bfloat16 [36864, 6144], P('ctx', 'head'), may hold values from -0.09375 to 0.09375
Outputs:
- layer_out: bfloat16 [8192, 6144], P('ctx', 'head')
Inputs may be any that keep to these rules, and one draw needn't show every extreme that they name: `expert_ids`: A row's two ids differ; within the 128 rows of one block no id is named by more than 10 rows.
All inputs are finite; a program needn't handle non-finite values.
Results may differ from a plain program's by a relative error of at most 0.008.
Values may be sent and summed in bfloat16 or wider, within the bound.
No kernel may reach another device: no remote copies, remote signals or barrier semaphores. Data moves between devices by JAX's collectives and lax.ppermute only.
A program may use at most 128 MiB of HBM per device.

v0:
```python
import jax
import jax.numpy as jnp
from jax import lax
from jax.sharding import Mesh, PartitionSpec as P

EXP = 8
MOST = 10
CTX = ("g", "q", "core")
epsilon = 1e-06
highest = lax.Precision.HIGHEST


def pack_state(factor, state):
    heads, dim, _ = state.shape
    extra = jnp.broadcast_to(factor[:, None, None], (heads, 8, dim))
    return jnp.concatenate([state, extra], axis=1)


def unpack_state(packed):
    dim = packed.shape[-1]
    return (packed[:, dim, 0], packed[:, :dim, :])


def prefix_scan(factor, state, axis, count):
    place = lax.axis_index(axis)

    def shift(value, distance):
        return lax.ppermute(value, axis, [(i, i + distance) for i in range(count - distance)])

    identity = pack_state(jnp.ones_like(factor), jnp.zeros_like(state))
    current = jnp.where(place >= 1, shift(pack_state(factor, state), 1), identity)
    distance = 1
    while distance < count:
        earlier_factor, earlier_state = unpack_state(shift(current, distance))
        later_factor, later_state = unpack_state(current)
        joined = pack_state(
            earlier_factor * later_factor, later_factor[:, None, None] * earlier_state + later_state
        )
        current = jnp.where(place >= distance, joined, current)
        distance *= 2
    return unpack_state(current)[1]


def body(
    queries,
    key_heads,
    value_heads,
    gate_logits,
    log_decay,
    attn_gain,
    out_weight,
    residual,
    norm_gain,
    router_weight,
    expert_ids,
    expert_gate,
    expert_up,
    expert_down,
):
    ctx_count = lax.axis_size(CTX)
    head_count = lax.axis_size("head")
    head_index = lax.axis_index("head")
    tok_rows = queries.shape[0]
    local_heads = log_decay.shape[1]
    head_dim = queries.shape[1] // local_heads
    model_width = residual.shape[1]
    share_width = model_width // head_count
    query_blocks = queries.reshape(tok_rows, local_heads, head_dim)
    key_blocks = key_heads.reshape(tok_rows, local_heads, head_dim)
    value_blocks = value_heads.reshape(tok_rows, local_heads, head_dim)
    cumulative = jnp.cumsum(log_decay, axis=0)
    block_total = cumulative[-1]
    keys_decayed = (
        key_blocks.astype(jnp.float32) * jnp.exp(block_total[None, :] - cumulative)[:, :, None]
    ).astype(jnp.bfloat16)
    local_state = jnp.einsum(
        "thd,the->hde", keys_decayed, value_blocks, preferred_element_type=jnp.float32
    )
    core = lax.axis_index("core")
    swap = [(0, 1), (1, 0)]
    factor = jnp.exp(block_total)
    partner_factor, partner_state = unpack_state(
        lax.ppermute(pack_state(factor, local_state), "core", swap)
    )
    first_factor = jnp.where(core == 0, factor, partner_factor)
    first_state = jnp.where(core == 0, local_state, partner_state)
    second_factor = jnp.where(core == 0, partner_factor, factor)
    second_state = jnp.where(core == 0, partner_state, local_state)
    chip_factor = first_factor * second_factor
    chip_state = second_factor[:, None, None] * first_state + second_state
    half = local_heads // 2
    half_factor = jnp.where(core == 0, chip_factor[:half], chip_factor[half:])
    half_state = jnp.where(core == 0, chip_state[:half], chip_state[half:])
    mine = prefix_scan(half_factor, half_state, ("g", "q"), ctx_count // 2)
    other = lax.ppermute(mine, "core", swap)
    chip_entering = jnp.concatenate(
        [jnp.where(core == 0, mine, other), jnp.where(core == 0, other, mine)], axis=0
    )
    entering = jnp.where(
        core == 0, chip_entering, first_factor[:, None, None] * chip_entering + first_state
    )
    sequence_offsets = jnp.arange(tok_rows)
    causal = (sequence_offsets[:, None] >= sequence_offsets[None, :])[None, :, :]
    cum_heads = cumulative.T
    decay_gaps = jnp.where(causal, cum_heads[:, :, None] - cum_heads[:, None, :], 0.0)
    scores = jnp.einsum(
        "thd,shd->hts", query_blocks, key_blocks, preferred_element_type=jnp.float32
    )
    attn_probs = jnp.where(causal, scores * jnp.exp(decay_gaps), 0.0).astype(jnp.bfloat16)
    within = jnp.einsum(
        "hts,shd->thd", attn_probs, value_blocks, preferred_element_type=jnp.float32
    )
    carried = jnp.einsum(
        "thd,hde->the", query_blocks.astype(jnp.float32), entering, precision=highest
    )
    attended = within + carried * jnp.exp(cumulative)[:, :, None]
    rms_scale = lax.rsqrt(jnp.mean(attended * attended, axis=-1, keepdims=True) + epsilon)
    gate_open = jax.nn.sigmoid(
        gate_logits.astype(jnp.float32).reshape(tok_rows, local_heads, head_dim)
    )
    attn_mixed = (
        attended * rms_scale * attn_gain.reshape(local_heads, head_dim) * gate_open
    ).astype(jnp.bfloat16)
    half_width = share_width // 2
    split_weight = out_weight.reshape(local_heads, -1, head_count, 2, half_width)
    mine = jnp.where(core == 0, split_weight[:, :, :, 0], split_weight[:, :, :, 1])
    theirs = jnp.where(core == 0, split_weight[:, :, :, 1], split_weight[:, :, :, 0])
    received = lax.ppermute(theirs, "core", swap)
    pair_rows = jnp.concatenate(
        [jnp.where(core == 0, mine, received), jnp.where(core == 0, received, mine)], axis=1
    )
    row_whole = lax.all_gather(pair_rows, ("g", "q"), axis=1, tiled=True)
    partner_mixed = lax.ppermute(attn_mixed, "core", swap)
    both_mixed = jnp.concatenate(
        [
            jnp.where(core == 0, attn_mixed, partner_mixed),
            jnp.where(core == 0, partner_mixed, attn_mixed),
        ],
        axis=0,
    )
    partial_sum = jnp.einsum(
        "thr,hrqd->tqd", both_mixed, row_whole, preferred_element_type=jnp.float32
    )
    scattered = lax.psum_scatter(
        partial_sum.astype(jnp.bfloat16), "head", scatter_dimension=1, tiled=True
    ).reshape(2, tok_rows, half_width)
    own_rows = jnp.where(core == 0, scattered[0], scattered[1])
    other_rows = lax.ppermute(jnp.where(core == 0, scattered[1], scattered[0]), "core", swap)
    projected = jnp.concatenate(
        [jnp.where(core == 0, own_rows, other_rows), jnp.where(core == 0, other_rows, own_rows)],
        axis=1,
    ).astype(jnp.float32)
    share_start = head_index * share_width
    residual_share = lax.dynamic_slice_in_dim(residual, share_start, share_width, 1)
    gain_share = lax.dynamic_slice_in_dim(norm_gain, share_start, share_width, 0)
    router_share = lax.dynamic_slice_in_dim(router_weight, share_start, share_width, 0)
    hidden_share = residual_share.astype(jnp.float32) + projected
    router_part = jnp.dot(
        hidden_share * gain_share[None, :], router_share.astype(jnp.float32), precision=highest
    )
    square_part = jnp.sum(hidden_share * hidden_share, axis=-1, keepdims=True)
    stats = lax.psum(jnp.concatenate([square_part, router_part], axis=1), "head")
    row_scale = lax.rsqrt(stats[:, :1] / model_width + epsilon)
    logits = stats[:, 1:] * row_scale
    normed_share = (hidden_share * row_scale * gain_share[None, :]).astype(jnp.bfloat16)
    columns = jnp.arange(router_weight.shape[1], dtype=jnp.int32)
    picked = jnp.sum(
        jnp.where(columns[None, None, :] == expert_ids[:, :, None], logits[:, None, :], 0.0),
        axis=-1,
    )
    route_gates = jax.nn.sigmoid(picked - picked[:, ::-1])
    route_ids = expert_ids.reshape(-1)
    onehot = (route_ids[:, None] == jnp.arange(EXP, dtype=jnp.int32)[None, :]).astype(jnp.int32)
    before_count = jnp.cumsum(onehot, axis=0) - onehot
    slot_index = jnp.sum(before_count * onehot, axis=1)
    slot_range = jnp.arange(MOST, dtype=jnp.int32)
    placed = (onehot.T[:, None, :] == 1) & (slot_index[None, None, :] == slot_range[None, :, None])
    chooser = (
        jnp.sum(placed.reshape(EXP, MOST, tok_rows, 2).astype(jnp.float32), axis=3)
        .astype(jnp.bfloat16)
        .reshape(EXP * MOST, tok_rows)
    )
    weighted = jnp.sum(
        (placed.astype(jnp.float32) * route_gates.reshape(-1)[None, None, :]).reshape(
            EXP, MOST, tok_rows, 2
        ),
        axis=3,
    )
    group = ctx_count // EXP
    packed = (
        jnp.dot(chooser, normed_share, preferred_element_type=jnp.float32)
        .astype(jnp.bfloat16)
        .reshape(EXP, MOST, share_width)
    )
    by_group = lax.all_to_all(packed, "g", split_axis=0, concat_axis=0, tiled=True)
    wide = lax.all_gather(by_group.reshape(EXP * MOST, share_width), "head", axis=1, tiled=True)
    own_parity = lax.all_gather(wide, "q", axis=0, tiled=False)
    other_parity = lax.ppermute(own_parity, "core", swap)
    pairs = group // 2
    halves = []
    for part in (own_parity, other_parity):
        part_rows = part.reshape(-1, model_width)
        gate_part = jnp.einsum(
            "rd,fd->rf", part_rows, expert_gate, preferred_element_type=jnp.float32
        )
        up_part = jnp.einsum("rd,fd->rf", part_rows, expert_up, preferred_element_type=jnp.float32)
        halves.append((jax.nn.silu(gate_part) * up_part).astype(jnp.bfloat16))
    hidden_units = jnp.concatenate(halves, axis=0)
    joined = lax.all_gather(hidden_units, "head", axis=1, tiled=True)
    partial_value = (
        jnp.dot(joined, expert_down, preferred_element_type=jnp.float32)
        .astype(jnp.bfloat16)
        .reshape(2, pairs, EXP, MOST, share_width)
    )
    pair_sum = (
        partial_value[0].astype(jnp.float32)
        + lax.ppermute(partial_value[1], "core", swap).astype(jnp.float32)
    ).astype(jnp.bfloat16)
    outgoing = pair_sum.transpose(1, 0, 2, 3).reshape(EXP * pairs, MOST, share_width)
    returned = lax.all_to_all(outgoing, ("g", "q"), split_axis=0, concat_axis=0, tiled=True)
    summed = jnp.sum(returned.astype(jnp.float32).reshape(EXP, pairs, MOST, share_width), axis=1)
    mixture = jnp.einsum("est,esd->td", weighted, summed, precision=highest)
    return (hidden_share + mixture).astype(jnp.bfloat16)


def solution(mesh):
    ctx_count = mesh.shape["ctx"]
    head_count = mesh.shape["head"]
    split = Mesh(
        mesh.devices.reshape(EXP, ctx_count // EXP // 2, 2, head_count), ("g", "q", "core", "head")
    )
    ctx = CTX
    return jax.shard_map(
        body,
        mesh=split,
        in_specs=(
            P(ctx, "head"),
            P(ctx, "head"),
            P(ctx, "head"),
            P(ctx, "head"),
            P(ctx, "head"),
            P("head"),
            P("head", ctx, None),
            P(ctx, None),
            P(),
            P(),
            P(ctx, None),
            P(ctx + ("head",), None),
            P(ctx + ("head",), None),
            P(ctx, "head"),
        ),
        out_specs=P(ctx, "head"),
        check_vma=False,
    )
```

profile of v0, /device:TPU:34, one launch (start us, length us, event | category | flops | bytes accessed | tf_op | source)
XLA Modules:
  0.0 408.5 jit_solution(14363872480596723360)
XLA Ops:
  6.5 1.2 reshape.223
  7.8 0.3 fusion.72
  8.0 0.4 broadcast_select_fusion.1
  8.6 1.3 collective-permute-done.9
  9.9 0.7 pad_maximum_fusion.6
  11.3 1.3 fusion.26
  12.6 0.9 pad_maximum_fusion
  13.7 1.9 collective-permute-done
  16.2 3.8 collective-permute-start.1
  20.0 6.7 %collective-permute-done.1 = f32[4,136,128]{2,1,0:T(8,128)S(1)} collective-permute-done((f32[4,136,128]{2,1,0:T(8,128)S(1)}, f32[4,136,128]{2,1,0:T(8,128)S(1)}, u32[]{:S(2)}, u32[]{:S(2)}) %collective-permute-start.1) | collective-permute-done | bytes 278560 | tf_op jit(solution)/shard_map/ppermute | solution.py:28
  26.9 3.8 collective-permute-start.2
  30.7 8.0 %collective-permute-done.2 = f32[4,136,128]{2,1,0:T(8,128)S(1)} collective-permute-done((f32[4,136,128]{2,1,0:T(8,128)S(1)}, f32[4,136,128]{2,1,0:T(8,128)S(1)}, u32[]{:S(2)}, u32[]{:S(2)}) %collective-permute-start.2) | collective-permute-done | bytes 278560 | tf_op jit(solution)/shard_map/ppermute | solution.py:28
  39.1 8.8 %collective-permute-start.3 = (f32[4,136,128]{2,1,0:T(8,128)S(1)}, f32[4,136,128]{2,1,0:T(8,128)S(1)}, u32[]{:S(2)}, u32[]{:S(2)}) collective-permute-start(f32[4,136,128]{2,1,0:T(8,128)S(1)} %maximum_select_fusion), channel_id=1, source_target_pairs={{0,16},{8,24},{16,32},{24,40},{32,48},{40,56},{48,64},{56,72},{64,... | collective-permute-start | bytes 835592 | tf_op jit(solution)/shard_map/ppermute | solution.py:28
  47.9 10.5 %collective-permute-done.3 = f32[4,136,128]{2,1,0:T(8,128)S(1)} collective-permute-done((f32[4,136,128]{2,1,0:T(8,128)S(1)}, f32[4,136,128]{2,1,0:T(8,128)S(1)}, u32[]{:S(2)}, u32[]{:S(2)}) %collective-permute-start.3) | collective-permute-done | bytes 278560 | tf_op jit(solution)/shard_map/ppermute | solution.py:28
  58.7 7.3 %collective-permute-start.4 = (f32[4,136,128]{2,1,0:T(8,128)S(1)}, f32[4,136,128]{2,1,0:T(8,128)S(1)}, u32[]{:S(2)}, u32[]{:S(2)}) collective-permute-start(f32[4,136,128]{2,1,0:T(8,128)S(1)} %maximum_select_fusion.1), channel_id=1, source_target_pairs={{0,32},{8,40},{16,48},{24,56},{32,64},{40,72},{48,80},{56,88},{64,... | collective-permute-start | bytes 835592 | tf_op jit(solution)/shard_map/ppermute | solution.py:28
  66.1 15.8 %collective-permute-done.4 = f32[4,136,128]{2,1,0:T(8,128)S(1)} collective-permute-done((f32[4,136,128]{2,1,0:T(8,128)S(1)}, f32[4,136,128]{2,1,0:T(8,128)S(1)}, u32[]{:S(2)}, u32[]{:S(2)}) %collective-permute-start.4) | collective-permute-done | bytes 278560 | tf_op jit(solution)/shard_map/ppermute | solution.py:28
  82.2 6.3 %collective-permute-start.5 = (f32[4,136,128]{2,1,0:T(8,128)S(1)}, f32[4,136,128]{2,1,0:T(8,128)S(1)}, u32[]{:S(2)}, u32[]{:S(2)}) collective-permute-start(f32[4,136,128]{2,1,0:T(8,128)S(1)} %maximum_select_fusion.2), channel_id=1, source_target_pairs={{0,64},{8,72},{16,80},{24,88},{32,96},{40,104},{48,112},{56,120},{... | collective-permute-start | bytes 835592 | tf_op jit(solution)/shard_map/ppermute | solution.py:28
  88.5 12.4 %collective-permute-done.5 = f32[4,136,128]{2,1,0:T(8,128)S(1)} collective-permute-done((f32[4,136,128]{2,1,0:T(8,128)S(1)}, f32[4,136,128]{2,1,0:T(8,128)S(1)}, u32[]{:S(2)}, u32[]{:S(2)}) %collective-permute-start.5) | collective-permute-done | bytes 278560 | tf_op jit(solution)/shard_map/ppermute | solution.py:28
  101.3 3.5 collective-permute-start.6
  104.9 0.9 copy.170
  105.8 3.8 collective-permute-done.6
  109.9 0.8 fusion.32
  110.8 0.2 copy.171
  111.0 1.5 collective-permute-done.7
  112.5 1.1 broadcast_select_fusion.7
  113.6 2.5 fusion.9
  116.1 1.6 multiply_reduce_fusion.1
  117.7 0.2 multiply_convert_fusion.1
  117.9 0.4 collective-permute-start.8
  118.3 1.4 collective-permute-done.8
  119.8 18.2 %bitcast_convert_fusion = bf16[256,4,768]{2,0,1:T(8,128)(2,1)} fusion(bf16[8,128,4,768]{3,0,2,1:T(8,128)(2,1)} %all-gather.4.cloned.1.call-done, bf16[128,8,128]{2,0,1:T(8,128)(2,1)S(1)} %get-tuple-element.25, bf16[128,8,128]{2,0,1:T(8,128)(2,1)S(1)} %get-tuple-element.24), kind=kOutput, calls=%fused_computation.4 | convolution fusion | flops 1612447744 | bytes 8388608 | tf_op jit(solution)/shard_map/thr,hrqd->tqd/dot_general | solution.py:141
  138.5 0.6 reduce-window.6
  139.1 0.2 slice_reduce_fusion
  139.7 0.8 dynamic_slice.10
  140.5 31.0 %reduce-scatter.2.cloned.1.call-done = bf16[256,1,768]{2,0,1:T(8,128)(2,1)} async-done(((bf16[256,4,768]{2,0,1:T(8,128)(2,1)}), bf16[256,1,768]{2,0,1:T(8,128)(2,1)}) %reduce-scatter.2.cloned.1.call-update) | async-done | bytes 393232 | tf_op jit(solution)/shard_map/reduce_scatter | solution.py:144
  171.4 1.0 select_bitcast_fusion
  172.6 1.4 collective-permute-done.10
  174.0 1.1 bitcast_select_fusion.1
  175.1 1.3 multiply_reduce_fusion
  176.4 1.6 fusion.12
  178.1 14.8 %psum.7 = f32[128,33]{0,1:T(8,128)S(1)} all-reduce(f32[128,33]{0,1:T(8,128)S(1)} %pad_maximum_fusion.8), channel_id=1, replica_groups=mesh['g'=8,'q'=4,'core'=2,'head'=4] {'head'}, use_global_device_ids=true, to_apply=%region_7.8 | all-reduce | flops 4224 | bytes 33792 | tf_op jit(solution)/shard_map/psum | solution.py:162
  193.0 0.6 fusion.50
  193.7 1.3 convolution_convert_fusion.1
  195.0 0.8 reshape.208
  195.8 22.9 %all_to_all.10 = bf16[8,10,1536]{2,1,0:T(8,128)(2,1)} all-to-all(bf16[8,10,1536]{2,1,0:T(8,128)(2,1)} %reshape.208), channel_id=1, replica_groups=mesh['g'=8,'q'=4,'core'=2,'head'=4] {'g'}, dimensions={0} | all-to-all | bytes 491520 | tf_op jit(solution)/shard_map/all_to_all | solution.py:195
  218.7 1.8 reshape.209
  220.5 16.9 %all_gather.16 = bf16[80,6144]{1,0:T(8,128)(2,1)} all-gather(bf16[80,1536]{1,0:T(8,128)(2,1)} %reshape.209), channel_id=1, replica_groups=mesh['g'=8,'q'=4,'core'=2,'head'=4] {'head'}, dimensions={1}, use_global_device_ids=true | all-gather | bytes 1228800 | tf_op jit(solution)/shard_map/all_gather | solution.py:196
  237.4 74.8 %all-gather.6.cloned.1.call-done = bf16[320,6144]{1,0:T(8,128)(2,1)} async-done(((bf16[80,6144]{1,0:T(8,128)(2,1)}), bf16[320,6144]{1,0:T(8,128)(2,1)}) %all-gather.6.cloned.1.call-update) | async-done | bytes 3932176 | tf_op jit(solution)/shard_map/all_gather | solution.py:197
  312.2 3.8 fusion.76
  316.1 1.6 fusion.11
  317.7 1.5 collective-permute-done.11
  319.2 1.6 fusion.77
  320.9 1.6 multiply_convert_fusion.5
  322.6 14.0 %all_gather.19 = bf16[640,576]{0,1:T(8,128)(2,1)S(1)} all-gather(bf16[640,144]{0,1:T(8,128)(2,1)S(1)} %pad_maximum_fusion.7), channel_id=1, replica_groups=mesh['g'=8,'q'=4,'core'=2,'head'=4] {'head'}, dimensions={1}, use_global_device_ids=true | all-gather | bytes 921600 | tf_op jit(solution)/shard_map/all_gather | solution.py:209
  336.6 1.7 convolution_convert_fusion
  338.3 1.8 fusion.71
  340.1 1.4 squeeze.5
  341.5 1.5 copy.180
  343.0 3.0 reshape.215
  346.0 2.5 fusion.6
  348.6 49.5 %all_to_all.11 = bf16[32,10,1536]{2,1,0:T(8,128)(2,1)S(1)} all-to-all(bf16[32,10,1536]{2,1,0:T(8,128)(2,1)S(1)} %bitcast.105), channel_id=1, replica_groups=mesh['g'=8,'q'=4,'core'=2,'head'=4] {'g','q'}, dimensions={0} | all-to-all | bytes 1966080 | tf_op jit(solution)/shard_map/all_to_all | solution.py:220
  398.1 0.3 convert_reduce_fusion
  398.4 0.6 copy-done.5
  399.1 2.8 fusion.3
  (118 shorter events, 5.1 us)
Async XLA Ops:
  6.5 330.0 %copy-start = (bf16[576,1536]{1,0:T(8,128)(2,1)S(1)}, bf16[576,1536]{1,0:T(8,128)(2,1)}, u32[]{:S(2)}) copy-start(bf16[576,1536]{1,0:T(8,128)(2,1)} %param.27) | copy-start | bytes 5308420
  6.5 4.2 %copy-start.17 = (f32[128,8]{0,1:T(8,128)S(1)}, f32[128,8]{0,1:T(8,128)}, u32[]{:S(2)}) copy-start(f32[128,8]{0,1:T(8,128)} %param.18) | copy-start | bytes 12292
  6.5 113.3 %all-gather.4.cloned.1.call-start = ((), (), s32[]{:S(2)}) async-start(), calls=%async_computation.3 | async-start | bytes 6488064 | tf_op jit(solution)/shard_map/all_gather | solution.py:132
  7.7 3.3 copy-start.12
  8.5 1.4 collective-permute-start.9
  10.6 160.8 %reduce-scatter.2.cloned.1.call-start = ((), (), s32[]{:S(2)}) async-start(), calls=%async_computation.4 | async-start | bytes 1966080 | tf_op jit(solution)/shard_map/reduce_scatter | solution.py:144
  11.3 1.4 copy-start.9
  13.5 2.2 collective-permute-start
  15.6 23.2 %copy-start.3 = (f32[8,136,128]{2,1,0:T(8,128)}, f32[8,136,128]{2,1,0:T(8,128)S(1)}, u32[]{:S(2)}) copy-start(f32[8,136,128]{2,1,0:T(8,128)S(1)} %collective-permute-done) | copy-start | bytes 1671172
  16.2 10.6 %collective-permute-start.1 = (f32[4,136,128]{2,1,0:T(8,128)S(1)}, f32[4,136,128]{2,1,0:T(8,128)S(1)}, u32[]{:S(2)}, u32[]{:S(2)}) collective-permute-start(f32[4,136,128]{2,1,0:T(8,128)S(1)} %pad_maximum_fusion.4), channel_id=1, source_target_pairs={{0,8},{8,16},{16,24},{24,32},{32,40},{40,48},{48,56},{56,64},{64,7... | collective-permute-start | bytes 835592 | tf_op jit(solution)/shard_map/ppermute | solution.py:28
  26.9 11.8 %collective-permute-start.2 = (f32[4,136,128]{2,1,0:T(8,128)S(1)}, f32[4,136,128]{2,1,0:T(8,128)S(1)}, u32[]{:S(2)}, u32[]{:S(2)}) collective-permute-start(f32[4,136,128]{2,1,0:T(8,128)S(1)} %broadcast_select_fusion.5), channel_id=1, source_target_pairs={{0,8},{8,16},{16,24},{24,32},{32,40},{40,48},{48,56},{56,64},{64,7... | collective-permute-start | bytes 835592 | tf_op jit(solution)/shard_map/ppermute | solution.py:28
  39.1 19.3 %collective-permute-start.3 = (f32[4,136,128]{2,1,0:T(8,128)S(1)}, f32[4,136,128]{2,1,0:T(8,128)S(1)}, u32[]{:S(2)}, u32[]{:S(2)}) collective-permute-start(f32[4,136,128]{2,1,0:T(8,128)S(1)} %maximum_select_fusion), channel_id=1, source_target_pairs={{0,16},{8,24},{16,32},{24,40},{32,48},{40,56},{48,64},{56,72},{64,... | collective-permute-start | bytes 835592 | tf_op jit(solution)/shard_map/ppermute | solution.py:28
  58.7 46.2 %copy-start.13 = (bf16[128,1024]{1,0:T(8,128)(2,1)S(1)}, bf16[128,1024]{1,0:T(8,128)(2,1)}, u32[]{:S(2)}) copy-start(bf16[128,1024]{1,0:T(8,128)(2,1)} %param.17) | copy-start | bytes 786436
  58.7 23.1 %collective-permute-start.4 = (f32[4,136,128]{2,1,0:T(8,128)S(1)}, f32[4,136,128]{2,1,0:T(8,128)S(1)}, u32[]{:S(2)}, u32[]{:S(2)}) collective-permute-start(f32[4,136,128]{2,1,0:T(8,128)S(1)} %maximum_select_fusion.1), channel_id=1, source_target_pairs={{0,32},{8,40},{16,48},{24,56},{32,64},{40,72},{48,80},{56,88},{64,... | collective-permute-start | bytes 835592 | tf_op jit(solution)/shard_map/ppermute | solution.py:28
  82.2 18.7 %collective-permute-start.5 = (f32[4,136,128]{2,1,0:T(8,128)S(1)}, f32[4,136,128]{2,1,0:T(8,128)S(1)}, u32[]{:S(2)}, u32[]{:S(2)}) collective-permute-start(f32[4,136,128]{2,1,0:T(8,128)S(1)} %maximum_select_fusion.2), channel_id=1, source_target_pairs={{0,64},{8,72},{16,80},{24,88},{32,96},{40,104},{48,112},{56,120},{... | collective-permute-start | bytes 835592 | tf_op jit(solution)/shard_map/ppermute | solution.py:28
  101.3 8.3 %collective-permute-start.6 = (f32[4,136,128]{2,1,0:T(8,128)S(1)}, f32[4,136,128]{2,1,0:T(8,128)S(1)}, u32[]{:S(2)}, u32[]{:S(2)}) collective-permute-start(f32[4,136,128]{2,1,0:T(8,128)S(1)} %maximum_select_fusion.3), channel_id=1, source_target_pairs={{0,128},{8,136},{16,144},{24,152},{32,160},{40,168},{48,176},{56,1... | collective-permute-start | bytes 835592 | tf_op jit(solution)/shard_map/ppermute | solution.py:28
  105.8 4.8 %copy-start.8 = (bf16[128,1024]{0,1:T(8,128)(2,1)S(1)}, bf16[128,1024]{0,1:T(8,128)(2,1)}, u32[]{:S(2)}) copy-start(bf16[128,1024]{0,1:T(8,128)(2,1)} %copy.170) | copy-start | bytes 786436
  110.6 1.9 collective-permute-start.7
  111.0 5.1 %copy-start.10 = (bf16[128,1024]{0,1:T(8,128)(2,1)S(1)}, bf16[128,1024]{0,1:T(8,128)(2,1)}, u32[]{:S(2)}) copy-start(bf16[128,1024]{0,1:T(8,128)(2,1)} %copy-done.9) | copy-start | bytes 786436
  111.0 5.1 %copy-start.11 = (bf16[128,1024]{1,0:T(8,128)(2,1)S(1)}, bf16[128,1024]{1,0:T(8,128)(2,1)}, u32[]{:S(2)}) copy-start(bf16[128,1024]{1,0:T(8,128)(2,1)} %param.14) | copy-start | bytes 786436
  113.6 4.1 %copy-start.16 = (f32[1024]{0:T(1024)S(1)}, f32[1024]{0:T(1024)}, u32[]{:S(2)}) copy-start(f32[1024]{0:T(1024)} %param.19) | copy-start | bytes 12292
  117.9 1.8 collective-permute-start.8
  119.8 18.3 %copy-start.15 = (s32[128,2]{0,1:T(2,128)S(1)}, s32[128,2]{0,1:T(2,128)}, u32[]{:S(2)}) copy-start(s32[128,2]{0,1:T(2,128)} %param.24) | copy-start | bytes 3076
  138.0 174.2 %all-gather.6.cloned.1.call-start = ((), (), s32[]{:S(2)}) async-start(), calls=%async_computation.5 | async-start | bytes 4915200 | tf_op jit(solution)/shard_map/all_gather | solution.py:197
  172.5 1.5 collective-permute-start.10
  175.1 19.9 %copy-start.4 = (bf16[128,768]{1,0:T(8,128)(2,1)}, bf16[128,768]{1,0:T(8,128)(2,1)S(1)}, u32[]{:S(2)}) copy-start(bf16[128,768]{1,0:T(8,128)(2,1)S(1)} %get-tuple-element.22) | copy-start | bytes 589828
  175.1 19.9 %copy-start.6 = (bf16[128,768]{1,0:T(8,128)(2,1)}, bf16[128,768]{1,0:T(8,128)(2,1)S(1)}, u32[]{:S(2)}) copy-start(bf16[128,768]{1,0:T(8,128)(2,1)S(1)} %get-tuple-element.23) | copy-start | bytes 589828
  195.8 116.4 %copy-start.1 = (bf16[144,6144]{1,0:T(8,128)(2,1)S(1)}, bf16[144,6144]{1,0:T(8,128)(2,1)}, u32[]{:S(2)}) copy-start(bf16[144,6144]{1,0:T(8,128)(2,1)} %param.25) | copy-start | bytes 5308420
  312.2 3.9 copy-start.2
  312.2 3.9 copy-start.18
  312.2 7.0 %collective-permute-start.11 = (bf16[4,80,6144]{2,1,0:T(8,128)(2,1)}, bf16[4,80,6144]{2,1,0:T(8,128)(2,1)S(1)}, u32[]{:S(2)}, u32[]{:S(2)}) collective-permute-start(bf16[4,80,6144]{2,1,0:T(8,128)(2,1)} %bitcast.106), channel_id=1, source_target_pairs={{0,4},{4,0},{1,5},{5,1},{2,6},{6,2},{3,7},{7,3},{8,12},{12,8},{9,1... | collective-permute-start | bytes 11796488 | tf_op jit(solution)/shard_map/ppermute | solution.py:198
  343.0 3.0 collective-permute-start.12
  398.1 0.9 copy-start.5
  398.1 1.0 copy-start.7
  398.1 1.0 copy-start.14
Sparse Core Ops, SparseCore 0:
  10.8 99.6 all-gather.3
  138.2 33.2 reduce-scatter.1
  237.5 74.6 all-gather.5
where the time goes:
time: 409 us; the launch traced here: 408 us
  waiting for transfers between devices  172 us (42%)
  blocking collectives  118 us (29%)
  matrix products  39.7 us (10%)
  starting transfers between devices  34.5 us (8%)
  other arithmetic  15.7 us (4%)
  local copies, waits for them, and re-layouts  14.7 us (4%)
  between operations  13.7 us (3%)
    all_gather x1, waiting for transfers between devices, body(): own_parity = lax.all_gather(wide, 'q', axis=0, tiled=False)  74.8 us
    ppermute x6, waiting for transfers between devices, shift(): lax.ppermute(value, axis, [(i, i + distance) for i in range(count - dista...  57.2 us
    all_to_all x1, blocking collectives, body(): lax.all_to_all(outgoing, ('g', 'q'), split_axis=0, concat_axis=0, tiled=T...  49.5 us
    ppermute x6, starting transfers between devices, shift(): lax.ppermute(value, axis, [(i, i + distance) for i in range(count - dista...  33.6 us
    reduce_scatter x1, waiting for transfers between devices, body(): lax.psum_scatter(partial_sum.astype(jnp.bfloat16), 'head', scatter_dimens...  31 us
    all_to_all x1, blocking collectives, body(): lax.all_to_all(packed, 'g', split_axis=0, concat_axis=0, tiled=True)  22.9 us
    dot_general x1, matrix products, body(): jnp.einsum('thr,hrqd->tqd', both_mixed, row_whole, preferred_element_type...  18.2 us
    all_gather x1, blocking collectives, body(): lax.all_gather(by_group.reshape(EXP * MOST, share_width), 'head', axis=1,...  16.9 us
  transfers between devices with their start and end apart: 16, of which 14 were waited for; matrix products, arithmetic and copies ran while one was open for 6% of the time, Pallas kernels for 0%

commit v1 on v0

--- a/solution.py
+++ b/solution.py
@@ -159,7 +159,9 @@
         hidden_share * gain_share[None, :], router_share.astype(jnp.float32), precision=highest
     )
     square_part = jnp.sum(hidden_share * hidden_share, axis=-1, keepdims=True)
-    stats = lax.psum(jnp.concatenate([square_part, router_part], axis=1), "head")
+    stats = jnp.sum(
+        lax.all_gather(jnp.concatenate([square_part, router_part], axis=1), "head"), axis=0
+    )
     row_scale = lax.rsqrt(stats[:, :1] / model_width + epsilon)
     logits = stats[:, 1:] * row_scale
     normed_share = (hidden_share * row_scale * gain_share[None, :]).astype(jnp.bfloat16)

time: 409 us -> 405 us (level)
  blocking collectives: 118 us -> 113 us
    psum x1 -> x0, blocking collectives: 14.8 us -> none  [body(): lax.psum(jnp.concatenate([square_part, router_part], axis=1), 'head')]
    all_gather x0 -> x1, blocking collectives: none -> 11.9 us  [body(): lax.all_gather(jnp.concatenate([square_part, router_part], axis=1), 'head')]
where the time goes in v1:
time: 405 us; the launch traced here: 404 us
  waiting for transfers between devices  172 us (42%)
  blocking collectives  113 us (28%)
  matrix products  39.7 us (10%)
  starting transfers between devices  34.5 us (9%)
  other arithmetic  15.7 us (4%)
  local copies, waits for them, and re-layouts  14.8 us (4%)
  between operations  13.7 us (3%)
    all_gather x1, waiting for transfers between devices, body(): own_parity = lax.all_gather(wide, 'q', axis=0, tiled=False)  75 us
    ppermute x6, waiting for transfers between devices, shift(): lax.ppermute(value, axis, [(i, i + distance) for i in range(count - dista...  57.2 us
    all_to_all x1, blocking collectives, body(): lax.all_to_all(outgoing, ('g', 'q'), split_axis=0, concat_axis=0, tiled=T...  49.5 us
    ppermute x6, starting transfers between devices, shift(): lax.ppermute(value, axis, [(i, i + distance) for i in range(count - dista...  33.6 us
    reduce_scatter x1, waiting for transfers between devices, body(): lax.psum_scatter(partial_sum.astype(jnp.bfloat16), 'head', scatter_dimens...  31 us
    all_to_all x1, blocking collectives, body(): lax.all_to_all(packed, 'g', split_axis=0, concat_axis=0, tiled=True)  23.1 us
    dot_general x1, matrix products, body(): jnp.einsum('thr,hrqd->tqd', both_mixed, row_whole, preferred_element_type...  18.2 us
    all_gather x1, blocking collectives, body(): lax.all_gather(by_group.reshape(EXP * MOST, share_width), 'head', axis=1,...  14.8 us
  transfers between devices with their start and end apart: 16, of which 14 were waited for; matrix products, arithmetic and copies ran while one was open for 6% of the time, Pallas kernels for 0%

profile of v1, /device:TPU:34, one launch (start us, length us, event | category | flops | bytes accessed | tf_op | source)
XLA Modules:
  0.0 404.0 jit_solution(5165751578406027457)
XLA Ops:
  6.5 1.2 reshape.224
  7.8 0.3 fusion.72
  8.0 0.4 broadcast_select_fusion.1
  8.6 1.3 collective-permute-done.9
  9.9 0.7 pad_maximum_fusion.6
  11.3 1.3 fusion.26
  12.6 0.9 pad_maximum_fusion
  13.7 1.9 collective-permute-done
  16.2 3.8 collective-permute-start.1
  20.0 6.7 %collective-permute-done.1 = f32[4,136,128]{2,1,0:T(8,128)S(1)} collective-permute-done((f32[4,136,128]{2,1,0:T(8,128)S(1)}, f32[4,136,128]{2,1,0:T(8,128)S(1)}, u32[]{:S(2)}, u32[]{:S(2)}) %collective-permute-start.1) | collective-permute-done | bytes 278560 | tf_op jit(solution)/shard_map/ppermute | solution.py:28
  26.9 3.8 collective-permute-start.2
  30.7 8.0 %collective-permute-done.2 = f32[4,136,128]{2,1,0:T(8,128)S(1)} collective-permute-done((f32[4,136,128]{2,1,0:T(8,128)S(1)}, f32[4,136,128]{2,1,0:T(8,128)S(1)}, u32[]{:S(2)}, u32[]{:S(2)}) %collective-permute-start.2) | collective-permute-done | bytes 278560 | tf_op jit(solution)/shard_map/ppermute | solution.py:28
  39.1 8.8 %collective-permute-start.3 = (f32[4,136,128]{2,1,0:T(8,128)S(1)}, f32[4,136,128]{2,1,0:T(8,128)S(1)}, u32[]{:S(2)}, u32[]{:S(2)}) collective-permute-start(f32[4,136,128]{2,1,0:T(8,128)S(1)} %maximum_select_fusion), channel_id=1, source_target_pairs={{0,16},{8,24},{16,32},{24,40},{32,48},{40,56},{48,64},{56,72},{64,... | collective-permute-start | bytes 835592 | tf_op jit(solution)/shard_map/ppermute | solution.py:28
  47.9 10.5 %collective-permute-done.3 = f32[4,136,128]{2,1,0:T(8,128)S(1)} collective-permute-done((f32[4,136,128]{2,1,0:T(8,128)S(1)}, f32[4,136,128]{2,1,0:T(8,128)S(1)}, u32[]{:S(2)}, u32[]{:S(2)}) %collective-permute-start.3) | collective-permute-done | bytes 278560 | tf_op jit(solution)/shard_map/ppermute | solution.py:28
  58.7 7.3 %collective-permute-start.4 = (f32[4,136,128]{2,1,0:T(8,128)S(1)}, f32[4,136,128]{2,1,0:T(8,128)S(1)}, u32[]{:S(2)}, u32[]{:S(2)}) collective-permute-start(f32[4,136,128]{2,1,0:T(8,128)S(1)} %maximum_select_fusion.1), channel_id=1, source_target_pairs={{0,32},{8,40},{16,48},{24,56},{32,64},{40,72},{48,80},{56,88},{64,... | collective-permute-start | bytes 835592 | tf_op jit(solution)/shard_map/ppermute | solution.py:28
  66.1 15.8 %collective-permute-done.4 = f32[4,136,128]{2,1,0:T(8,128)S(1)} collective-permute-done((f32[4,136,128]{2,1,0:T(8,128)S(1)}, f32[4,136,128]{2,1,0:T(8,128)S(1)}, u32[]{:S(2)}, u32[]{:S(2)}) %collective-permute-start.4) | collective-permute-done | bytes 278560 | tf_op jit(solution)/shard_map/ppermute | solution.py:28
  82.2 6.3 %collective-permute-start.5 = (f32[4,136,128]{2,1,0:T(8,128)S(1)}, f32[4,136,128]{2,1,0:T(8,128)S(1)}, u32[]{:S(2)}, u32[]{:S(2)}) collective-permute-start(f32[4,136,128]{2,1,0:T(8,128)S(1)} %maximum_select_fusion.2), channel_id=1, source_target_pairs={{0,64},{8,72},{16,80},{24,88},{32,96},{40,104},{48,112},{56,120},{... | collective-permute-start | bytes 835592 | tf_op jit(solution)/shard_map/ppermute | solution.py:28
  88.5 12.4 %collective-permute-done.5 = f32[4,136,128]{2,1,0:T(8,128)S(1)} collective-permute-done((f32[4,136,128]{2,1,0:T(8,128)S(1)}, f32[4,136,128]{2,1,0:T(8,128)S(1)}, u32[]{:S(2)}, u32[]{:S(2)}) %collective-permute-start.5) | collective-permute-done | bytes 278560 | tf_op jit(solution)/shard_map/ppermute | solution.py:28
  101.3 3.5 collective-permute-start.6
  104.9 0.9 copy.170
  105.8 3.8 collective-permute-done.6
  109.9 0.8 fusion.32
  110.8 0.2 copy.171
  111.0 1.5 collective-permute-done.7
  112.5 1.1 broadcast_select_fusion.7
  113.6 2.5 fusion.9
  116.1 1.6 multiply_reduce_fusion.1
  117.7 0.2 multiply_convert_fusion.1
  117.9 0.4 collective-permute-start.8
  118.3 1.4 collective-permute-done.8
  119.8 18.2 %bitcast_convert_fusion = bf16[256,4,768]{2,0,1:T(8,128)(2,1)} fusion(bf16[8,128,4,768]{3,0,2,1:T(8,128)(2,1)} %all-gather.5.cloned.1.call-done, bf16[128,8,128]{2,0,1:T(8,128)(2,1)S(1)} %get-tuple-element.25, bf16[128,8,128]{2,0,1:T(8,128)(2,1)S(1)} %get-tuple-element.24), kind=kOutput, calls=%fused_computation.4 | convolution fusion | flops 1612447744 | bytes 8388608 | tf_op jit(solution)/shard_map/thr,hrqd->tqd/dot_general | solution.py:141
  138.5 0.6 reduce-window.6
  139.1 0.2 slice_reduce_fusion
  139.7 0.8 dynamic_slice.10
  140.5 31.0 %reduce-scatter.2.cloned.1.call-done = bf16[256,1,768]{2,0,1:T(8,128)(2,1)} async-done(((bf16[256,4,768]{2,0,1:T(8,128)(2,1)}), bf16[256,1,768]{2,0,1:T(8,128)(2,1)}) %reduce-scatter.2.cloned.1.call-update) | async-done | bytes 393232 | tf_op jit(solution)/shard_map/reduce_scatter | solution.py:144
  171.4 1.0 select_bitcast_fusion
  172.6 1.4 collective-permute-done.10
  174.0 1.1 bitcast_select_fusion.1
  175.1 1.3 multiply_reduce_fusion
  176.4 1.6 fusion.12
  178.1 11.9 %all-gather = f32[512,33]{0,1:T(8,128)S(1)} all-gather(f32[128,33]{0,1:T(8,128)S(1)} %pad_maximum_fusion.8), channel_id=2, replica_groups=mesh['g'=8,'q'=4,'core'=2,'head'=4] {'head'}, dimensions={0}, use_global_device_ids=true | all-gather | bytes 84480 | tf_op jit(solution)/shard_map/all_gather | solution.py:163
  190.2 0.6 fusion.50
  190.8 1.3 convolution_convert_fusion.1
  192.2 0.8 reshape.208
  193.0 23.1 %all_to_all.10 = bf16[8,10,1536]{2,1,0:T(8,128)(2,1)} all-to-all(bf16[8,10,1536]{2,1,0:T(8,128)(2,1)} %reshape.208), channel_id=1, replica_groups=mesh['g'=8,'q'=4,'core'=2,'head'=4] {'g'}, dimensions={0} | all-to-all | bytes 491520 | tf_op jit(solution)/shard_map/all_to_all | solution.py:197
  216.1 1.8 reshape.209
  217.9 14.8 %all_gather.24 = bf16[80,6144]{1,0:T(8,128)(2,1)} all-gather(bf16[80,1536]{1,0:T(8,128)(2,1)} %reshape.209), channel_id=1, replica_groups=mesh['g'=8,'q'=4,'core'=2,'head'=4] {'head'}, dimensions={1}, use_global_device_ids=true | all-gather | bytes 1228800 | tf_op jit(solution)/shard_map/all_gather | solution.py:198
  232.8 75.0 %all-gather.7.cloned.1.call-done = bf16[320,6144]{1,0:T(8,128)(2,1)} async-done(((bf16[80,6144]{1,0:T(8,128)(2,1)}), bf16[320,6144]{1,0:T(8,128)(2,1)}) %all-gather.7.cloned.1.call-update) | async-done | bytes 3932176 | tf_op jit(solution)/shard_map/all_gather | solution.py:199
  307.7 3.8 fusion.76
  311.6 1.6 fusion.11
  313.2 1.5 collective-permute-done.11
  314.7 1.6 fusion.77
  316.4 1.6 multiply_convert_fusion.5
  318.1 14.0 %all_gather.27 = bf16[640,576]{0,1:T(8,128)(2,1)S(1)} all-gather(bf16[640,144]{0,1:T(8,128)(2,1)S(1)} %pad_maximum_fusion.7), channel_id=1, replica_groups=mesh['g'=8,'q'=4,'core'=2,'head'=4] {'head'}, dimensions={1}, use_global_device_ids=true | all-gather | bytes 921600 | tf_op jit(solution)/shard_map/all_gather | solution.py:211
  332.1 1.7 convolution_convert_fusion
  333.8 1.8 fusion.71
  335.6 1.4 squeeze.5
  337.0 1.5 copy.180
  338.5 3.0 reshape.215
  341.5 2.5 fusion.6
  344.1 49.5 %all_to_all.11 = bf16[32,10,1536]{2,1,0:T(8,128)(2,1)S(1)} all-to-all(bf16[32,10,1536]{2,1,0:T(8,128)(2,1)S(1)} %bitcast.107), channel_id=1, replica_groups=mesh['g'=8,'q'=4,'core'=2,'head'=4] {'g','q'}, dimensions={0} | all-to-all | bytes 1966080 | tf_op jit(solution)/shard_map/all_to_all | solution.py:222
  393.6 0.3 convert_reduce_fusion
  393.9 0.6 copy-done.5
  394.7 2.8 fusion.3
  (120 shorter events, 5.1 us)
Async XLA Ops:
  6.5 325.6 %copy-start = (bf16[576,1536]{1,0:T(8,128)(2,1)S(1)}, bf16[576,1536]{1,0:T(8,128)(2,1)}, u32[]{:S(2)}) copy-start(bf16[576,1536]{1,0:T(8,128)(2,1)} %param.27) | copy-start | bytes 5308420
  6.5 4.2 %copy-start.17 = (f32[128,8]{0,1:T(8,128)S(1)}, f32[128,8]{0,1:T(8,128)}, u32[]{:S(2)}) copy-start(f32[128,8]{0,1:T(8,128)} %param.18) | copy-start | bytes 12292
  6.5 113.3 %all-gather.5.cloned.1.call-start = ((), (), s32[]{:S(2)}) async-start(), calls=%async_computation.3 | async-start | bytes 6488064 | tf_op jit(solution)/shard_map/all_gather | solution.py:132
  7.7 3.3 copy-start.12
  8.5 1.4 collective-permute-start.9
  10.6 160.8 %reduce-scatter.2.cloned.1.call-start = ((), (), s32[]{:S(2)}) async-start(), calls=%async_computation.4 | async-start | bytes 1966080 | tf_op jit(solution)/shard_map/reduce_scatter | solution.py:144
  11.3 1.4 copy-start.9
  13.5 2.2 collective-permute-start
  15.6 23.2 %copy-start.3 = (f32[8,136,128]{2,1,0:T(8,128)}, f32[8,136,128]{2,1,0:T(8,128)S(1)}, u32[]{:S(2)}) copy-start(f32[8,136,128]{2,1,0:T(8,128)S(1)} %collective-permute-done) | copy-start | bytes 1671172
  16.2 10.6 %collective-permute-start.1 = (f32[4,136,128]{2,1,0:T(8,128)S(1)}, f32[4,136,128]{2,1,0:T(8,128)S(1)}, u32[]{:S(2)}, u32[]{:S(2)}) collective-permute-start(f32[4,136,128]{2,1,0:T(8,128)S(1)} %pad_maximum_fusion.4), channel_id=1, source_target_pairs={{0,8},{8,16},{16,24},{24,32},{32,40},{40,48},{48,56},{56,64},{64,7... | collective-permute-start | bytes 835592 | tf_op jit(solution)/shard_map/ppermute | solution.py:28
  26.9 11.8 %collective-permute-start.2 = (f32[4,136,128]{2,1,0:T(8,128)S(1)}, f32[4,136,128]{2,1,0:T(8,128)S(1)}, u32[]{:S(2)}, u32[]{:S(2)}) collective-permute-start(f32[4,136,128]{2,1,0:T(8,128)S(1)} %broadcast_select_fusion.5), channel_id=1, source_target_pairs={{0,8},{8,16},{16,24},{24,32},{32,40},{40,48},{48,56},{56,64},{64,7... | collective-permute-start | bytes 835592 | tf_op jit(solution)/shard_map/ppermute | solution.py:28
  39.1 19.3 %collective-permute-start.3 = (f32[4,136,128]{2,1,0:T(8,128)S(1)}, f32[4,136,128]{2,1,0:T(8,128)S(1)}, u32[]{:S(2)}, u32[]{:S(2)}) collective-permute-start(f32[4,136,128]{2,1,0:T(8,128)S(1)} %maximum_select_fusion), channel_id=1, source_target_pairs={{0,16},{8,24},{16,32},{24,40},{32,48},{40,56},{48,64},{56,72},{64,... | collective-permute-start | bytes 835592 | tf_op jit(solution)/shard_map/ppermute | solution.py:28
  58.7 46.2 %copy-start.13 = (bf16[128,1024]{1,0:T(8,128)(2,1)S(1)}, bf16[128,1024]{1,0:T(8,128)(2,1)}, u32[]{:S(2)}) copy-start(bf16[128,1024]{1,0:T(8,128)(2,1)} %param.17) | copy-start | bytes 786436
  58.7 23.1 %collective-permute-start.4 = (f32[4,136,128]{2,1,0:T(8,128)S(1)}, f32[4,136,128]{2,1,0:T(8,128)S(1)}, u32[]{:S(2)}, u32[]{:S(2)}) collective-permute-start(f32[4,136,128]{2,1,0:T(8,128)S(1)} %maximum_select_fusion.1), channel_id=1, source_target_pairs={{0,32},{8,40},{16,48},{24,56},{32,64},{40,72},{48,80},{56,88},{64,... | collective-permute-start | bytes 835592 | tf_op jit(solution)/shard_map/ppermute | solution.py:28
  82.2 18.7 %collective-permute-start.5 = (f32[4,136,128]{2,1,0:T(8,128)S(1)}, f32[4,136,128]{2,1,0:T(8,128)S(1)}, u32[]{:S(2)}, u32[]{:S(2)}) collective-permute-start(f32[4,136,128]{2,1,0:T(8,128)S(1)} %maximum_select_fusion.2), channel_id=1, source_target_pairs={{0,64},{8,72},{16,80},{24,88},{32,96},{40,104},{48,112},{56,120},{... | collective-permute-start | bytes 835592 | tf_op jit(solution)/shard_map/ppermute | solution.py:28
  101.3 8.3 %collective-permute-start.6 = (f32[4,136,128]{2,1,0:T(8,128)S(1)}, f32[4,136,128]{2,1,0:T(8,128)S(1)}, u32[]{:S(2)}, u32[]{:S(2)}) collective-permute-start(f32[4,136,128]{2,1,0:T(8,128)S(1)} %maximum_select_fusion.3), channel_id=1, source_target_pairs={{0,128},{8,136},{16,144},{24,152},{32,160},{40,168},{48,176},{56,1... | collective-permute-start | bytes 835592 | tf_op jit(solution)/shard_map/ppermute | solution.py:28
  105.8 4.8 %copy-start.8 = (bf16[128,1024]{0,1:T(8,128)(2,1)S(1)}, bf16[128,1024]{0,1:T(8,128)(2,1)}, u32[]{:S(2)}) copy-start(bf16[128,1024]{0,1:T(8,128)(2,1)} %copy.170) | copy-start | bytes 786436
  110.6 1.9 collective-permute-start.7
  111.0 5.1 %copy-start.10 = (bf16[128,1024]{0,1:T(8,128)(2,1)S(1)}, bf16[128,1024]{0,1:T(8,128)(2,1)}, u32[]{:S(2)}) copy-start(bf16[128,1024]{0,1:T(8,128)(2,1)} %copy-done.9) | copy-start | bytes 786436
  111.0 5.1 %copy-start.11 = (bf16[128,1024]{1,0:T(8,128)(2,1)S(1)}, bf16[128,1024]{1,0:T(8,128)(2,1)}, u32[]{:S(2)}) copy-start(bf16[128,1024]{1,0:T(8,128)(2,1)} %param.14) | copy-start | bytes 786436
  113.6 4.1 %copy-start.16 = (f32[1024]{0:T(1024)S(1)}, f32[1024]{0:T(1024)}, u32[]{:S(2)}) copy-start(f32[1024]{0:T(1024)} %param.19) | copy-start | bytes 12292
  117.9 1.8 collective-permute-start.8
  119.8 18.3 %copy-start.15 = (s32[128,2]{0,1:T(2,128)S(1)}, s32[128,2]{0,1:T(2,128)}, u32[]{:S(2)}) copy-start(s32[128,2]{0,1:T(2,128)} %param.24) | copy-start | bytes 3076
  138.0 169.7 %all-gather.7.cloned.1.call-start = ((), (), s32[]{:S(2)}) async-start(), calls=%async_computation.5 | async-start | bytes 4915200 | tf_op jit(solution)/shard_map/all_gather | solution.py:199
  172.5 1.5 collective-permute-start.10
  175.1 17.1 %copy-start.4 = (bf16[128,768]{1,0:T(8,128)(2,1)}, bf16[128,768]{1,0:T(8,128)(2,1)S(1)}, u32[]{:S(2)}) copy-start(bf16[128,768]{1,0:T(8,128)(2,1)S(1)} %get-tuple-element.22) | copy-start | bytes 589828
  175.1 17.1 %copy-start.6 = (bf16[128,768]{1,0:T(8,128)(2,1)}, bf16[128,768]{1,0:T(8,128)(2,1)S(1)}, u32[]{:S(2)}) copy-start(bf16[128,768]{1,0:T(8,128)(2,1)S(1)} %get-tuple-element.23) | copy-start | bytes 589828
  193.0 114.7 %copy-start.1 = (bf16[144,6144]{1,0:T(8,128)(2,1)S(1)}, bf16[144,6144]{1,0:T(8,128)(2,1)}, u32[]{:S(2)}) copy-start(bf16[144,6144]{1,0:T(8,128)(2,1)} %param.25) | copy-start | bytes 5308420
  307.7 3.9 copy-start.2
  307.7 3.9 copy-start.18
  307.7 7.0 %collective-permute-start.11 = (bf16[4,80,6144]{2,1,0:T(8,128)(2,1)}, bf16[4,80,6144]{2,1,0:T(8,128)(2,1)S(1)}, u32[]{:S(2)}, u32[]{:S(2)}) collective-permute-start(bf16[4,80,6144]{2,1,0:T(8,128)(2,1)} %bitcast.108), channel_id=1, source_target_pairs={{0,4},{4,0},{1,5},{5,1},{2,6},{6,2},{3,7},{7,3},{8,12},{12,8},{9,1... | collective-permute-start | bytes 11796488 | tf_op jit(solution)/shard_map/ppermute | solution.py:200
  338.5 3.0 collective-permute-start.12
  393.6 0.9 copy-start.5
  393.6 1.0 copy-start.7
  393.6 1.0 copy-start.14
Sparse Core Ops, SparseCore 0:
  10.8 99.6 all-gather.4
  138.2 33.2 reduce-scatter.1
  232.9 74.7 all-gather.6
